TPU v7x, 32 devices: a whole 2x2x4 slice. The times are simulated.
32 devices in a mesh: req: 8 (over y, x, core), tp: 4 (over z).
Axes of the slice: x: 2, y: 2, z: 4, core: 2. Of those that a mesh axis runs over, the one named last changes fastest.
Arguments:
- residual: bfloat16 [2048, 2048], P('req', 'tp'), may hold values from -0.29882812 to 0.29882812
- queries: bfloat16 [2048, 1280], P('req', 'tp'), may hold values from -6 to 6
- suffix_kv: bfloat16 [2048, 4, 256], P('req', 'tp'), may hold values from -4 to 4
- prefix_cache: bfloat16 [8192, 4, 256], P('req', 'tp'), may hold values from -6 to 6
- out_weight: bfloat16 [1280, 2048], P('tp'), may hold values from -0.15625 to 0.15625
- norm_gain: bfloat16 [2048], replicated, may hold values from 0.5 to 1.5
- next_query_weight: bfloat16 [2048, 1280], P(None, 'tp'), may hold values from -0.125 to 0.125
- lengths: int32 [8, 4], P('req'), may hold values from 1 to 128, 256 in all within a row
- tenant: int32 [8, 4], P('req'), may hold values from 0 to 3
- owners: int32 [4], replicated, may hold values from 0 to 7, as said below
Outputs:
- new_residual: bfloat16 [2048, 2048], P('req', 'tp')
- next_queries: bfloat16 [2048, 1280], P('req', 'tp')
Inputs may be any that keep to these rules, and one draw needn't show every extreme that they name: `lengths`: each device's 4 requests fill its 256 rows in order. `owners`: distinct.
All inputs are finite; a program needn't handle non-finite values.
Results may differ from a plain program's by a relative error of at most 0.0065.
Values may be sent and summed in bfloat16 or wider, within the bound.
No kernel may reach another device: no remote copies, remote signals or barrier semaphores. Data moves between devices by JAX's collectives and lax.ppermute only.
A program may use at most 64 MiB of HBM per device.

v0:
```python
import jax
import jax.numpy as jnp
from jax import lax
from jax.sharding import PartitionSpec as P

QH = 20
KVH = 5
HD = 64
TENANTS = 4
GATHER_SLOTS_MAX = 16


def from_root(block, axis, source):
    block = jnp.where(lax.axis_index(axis) == source, block, jnp.zeros_like(block))
    return lax.psum(block, axis)


def pick_heads(pair_rows, select):
    split_pair = pair_rows.reshape(pair_rows.shape[0], 2, 2, HD)
    key_heads = jnp.einsum(
        "njd,hj->nhd", split_pair[:, :, 0], select, preferred_element_type=jnp.float32
    ).astype(jnp.bfloat16)
    value_heads = jnp.einsum(
        "njd,hj->nhd", split_pair[:, :, 1], select, preferred_element_type=jnp.float32
    ).astype(jnp.bfloat16)
    return (key_heads, value_heads)


def every_slot_of(part, n_req):
    return lax.all_gather(part, "req", axis=0, tiled=True)


def slots_of_tenants(part, every_slot, owners, n_req):
    slot_rows = part.shape[0]
    if n_req <= GATHER_SLOTS_MAX:
        return [
            lax.dynamic_slice_in_dim(every_slot, owners[tenant_id] * slot_rows, slot_rows, 0)
            for tenant_id in range(TENANTS)
        ]
    return [from_root(part, "req", owners[tenant_id]) for tenant_id in range(TENANTS)]


def pick_part(part_rows, select):
    return jnp.einsum("njd,hj->nhd", part_rows, select, preferred_element_type=jnp.float32).astype(
        jnp.bfloat16
    )


def shifted(block, shift, n_tp):
    pairs = [(source, (source + shift) % n_tp) for source in range(n_tp)]
    return lax.ppermute(block, "tp", pairs)


def local(
    residual,
    queries,
    suffix_kv,
    prefix_cache,
    out_weight,
    norm_gain,
    next_query_weight,
    lengths,
    tenant,
    owners,
    n_req,
    n_tp,
):
    row_count = queries.shape[0]
    head_count = queries.shape[1] // HD
    width = residual.shape[1]
    tp_index = lax.axis_index("tp")
    weight_pieces = []
    for shift in range(n_tp):
        target = (tp_index + shift) % n_tp
        piece = lax.dynamic_slice_in_dim(out_weight, target * width, width, 1)
        weight_pieces.append(piece if shift == 0 else shifted(piece, shift, n_tp))
    head_ids = tp_index * head_count + jnp.arange(head_count, dtype=jnp.int32)
    pair_ids = head_ids // (QH // KVH) - tp_index
    select = (pair_ids[:, None] == jnp.arange(2, dtype=jnp.int32)[None, :]).astype(jnp.bfloat16)
    req_lengths = lengths[0]
    req_tenant = tenant[0]
    req_ends = jnp.cumsum(req_lengths)
    req_starts = req_ends - req_lengths
    position = jnp.arange(row_count, dtype=jnp.int32)
    request_ids = jnp.sum((position[:, None] >= req_ends[None, :]).astype(jnp.int32), axis=1)
    member = request_ids[:, None] == jnp.arange(req_lengths.shape[0], dtype=jnp.int32)[None, :]
    row_start = jnp.sum(jnp.where(member, req_starts[None, :], 0), axis=1)
    row_tenant = jnp.sum(jnp.where(member, req_tenant[None, :], 0), axis=1)
    score_scale = HD ** (-0.5)
    query_heads = queries.reshape(row_count, head_count, HD)
    suffix_keys, suffix_values = pick_heads(suffix_kv.reshape(row_count, -1), select)
    suffix_scores = (
        jnp.einsum("rhd,khd->hrk", query_heads, suffix_keys, preferred_element_type=jnp.float32)
        * score_scale
    )
    suffix_mask = (
        (position[None, :] >= row_start[:, None]) & (position[None, :] <= position[:, None])
    )[None]
    own_slot = prefix_cache.reshape(prefix_cache.shape[0], 2, 2, HD)
    own_keys = own_slot[:, :, 0]
    own_values = own_slot[:, :, 1]
    if n_req <= GATHER_SLOTS_MAX:
        every_key = every_slot_of(own_keys, n_req)
        own_values, every_key = lax.optimization_barrier((own_values, every_key))
        every_value = every_slot_of(own_values, n_req)
    else:
        every_key = every_value = None
    key_blocks = slots_of_tenants(own_keys, every_key, owners, n_req)
    value_blocks = slots_of_tenants(own_values, every_value, owners, n_req)
    picked = [
        (pick_part(key_rows, select), pick_part(value_rows, select))
        for key_rows, value_rows in zip(key_blocks, value_blocks)
    ]
    row_top = jnp.max(jnp.where(suffix_mask, suffix_scores, -jnp.inf), axis=2)
    for tenant_id in range(TENANTS):
        tenant_mask = (row_tenant == tenant_id)[None, :, None]
        prefix_scores = (
            jnp.einsum(
                "rhd,phd->hrp",
                query_heads,
                picked[tenant_id][0],
                preferred_element_type=jnp.float32,
            )
            * score_scale
        )
        row_top = jnp.maximum(
            row_top, jnp.max(jnp.where(tenant_mask, prefix_scores, -jnp.inf), axis=2)
        )
    suffix_weights = jnp.where(suffix_mask, jnp.exp(suffix_scores - row_top[:, :, None]), 0.0)
    denominator = jnp.sum(suffix_weights, axis=2)
    accumulated = jnp.einsum(
        "hrk,khd->rhd",
        suffix_weights.astype(jnp.bfloat16),
        suffix_values,
        preferred_element_type=jnp.float32,
    )
    for tenant_id in range(TENANTS):
        tenant_mask = (row_tenant == tenant_id)[None, :, None]
        prefix_scores = (
            jnp.einsum(
                "rhd,phd->hrp",
                query_heads,
                picked[tenant_id][0],
                preferred_element_type=jnp.float32,
            )
            * score_scale
        )
        prefix_weights = jnp.where(tenant_mask, jnp.exp(prefix_scores - row_top[:, :, None]), 0.0)
        denominator = denominator + jnp.sum(prefix_weights, axis=2)
        accumulated = accumulated + jnp.einsum(
            "hrp,phd->rhd",
            prefix_weights.astype(jnp.bfloat16),
            picked[tenant_id][1],
            preferred_element_type=jnp.float32,
        )
    attended = (
        (accumulated / jnp.transpose(denominator)[:, :, None])
        .astype(jnp.bfloat16)
        .reshape(row_count, -1)
    )
    projected = jnp.dot(attended, weight_pieces[0], preferred_element_type=jnp.float32)
    for shift in range(1, n_tp):
        head_block = shifted(attended, shift, n_tp)
        projected = projected + jnp.dot(
            head_block, weight_pieces[shift], preferred_element_type=jnp.float32
        )
    new_residual = (residual.astype(jnp.float32) + projected).astype(jnp.bfloat16)
    full_new = lax.all_gather(new_residual, "tp", axis=1, tiled=True)
    widened = full_new.astype(jnp.float32)
    mean_square = jnp.mean(widened * widened, axis=1, keepdims=True)
    normed = (widened * lax.rsqrt(mean_square + 1e-05) * norm_gain.astype(jnp.float32)).astype(
        jnp.bfloat16
    )
    next_sums = jnp.dot(normed, next_query_weight, preferred_element_type=jnp.float32)
    return (new_residual, next_sums.astype(jnp.bfloat16))


def solution(mesh):
    n_req = mesh.shape["req"]
    n_tp = mesh.shape["tp"]

    def body(*args):
        return local(*args, n_req=n_req, n_tp=n_tp)

    return jax.shard_map(
        body,
        mesh=mesh,
        in_specs=(
            P("req", "tp"),
            P("req", "tp"),
            P("req", "tp", None),
            P("req", "tp", None),
            P("tp", None),
            P(),
            P(None, "tp"),
            P("req", None),
            P("req", None),
            P(),
        ),
        out_specs=(P("req", "tp"), P("req", "tp")),
        check_vma=False,
    )
```

profile of v0, /device:TPU:0, one launch (start us, length us, event | category | flops | bytes accessed | tf_op | source)
XLA Modules:
  0.0 150.9 jit_solution(15637092772348222072)
XLA Ops:
  7.2 1.4 copy.28
  9.5 2.2 %constant_dynamic-slice_fusion.1 = (bf16[320,512]{1,0:T(8,128)(2,1)}, bf16[320,512]{1,0:T(8,128)(2,1)}, bf16[320,512]{1,0:T(8,128)(2,1)}) fusion(bf16[320,2048]{1,0:T(8,128)(2,1)} %param.14, s32[]{:T(128)S(6)} %select_n.137, s32[]{:T(128)S(6)} %select_n.135, s32[]{:T(128)S(6)} %select_n.139), kind=kLoop, calls=%fused_computation.113 | loop fusion | bytes 1966092 | tf_op jit(solution)/shard_map/dynamic_slice | solution.py:75
  11.7 3.0 %collective-permute-start.1 = (bf16[320,512]{1,0:T(8,128)(2,1)}, bf16[320,512]{1,0:T(8,128)(2,1)}, u32[]{:S(2)}, u32[]{:S(2)}) collective-permute-start(bf16[320,512]{1,0:T(8,128)(2,1)} %get-tuple-element.13), channel_id=1, source_target_pairs={{0,1},{1,2},{2,3},{3,0},{4,5},{5,6},{6,7},{7,4},{8,9},{9,10},{10,1... | collective-permute-start | bytes 983048 | tf_op jit(solution)/shard_map/ppermute | solution.py:51
  14.7 2.0 %collective-permute-start.5 = (bf16[320,512]{1,0:T(8,128)(2,1)}, bf16[320,512]{1,0:T(8,128)(2,1)}, u32[]{:S(2)}, u32[]{:S(2)}) collective-permute-start(bf16[320,512]{1,0:T(8,128)(2,1)} %get-tuple-element.14), channel_id=1, source_target_pairs={{0,3},{1,0},{2,1},{3,2},{4,7},{5,4},{6,5},{7,6},{8,11},{9,8},{10,9... | collective-permute-start | bytes 983048 | tf_op jit(solution)/shard_map/ppermute | solution.py:51
  17.7 1.5 fusion.108
  26.9 14.2 %all-gather.9.cloned.1.call-done = bf16[8192,2,1,64]{0,3,2,1:T(8,128)(2,1)} async-done(((bf16[1024,2,1,64]{0,3,2,1:T(8,128)(2,1)}), bf16[8192,2,1,64]{0,3,2,1:T(8,128)(2,1)}) %all-gather.9.cloned.1.call-update) | async-done | bytes 2097168 | tf_op jit(solution)/shard_map/all_gather | solution.py:30
  41.1 3.8 %copy.29 = bf16[8192,2,64]{0,1,2:T(2,128)(2,1)S(1)} copy(bf16[8192,2,64]{0,2,1:T(8,128)(2,1)} %bitcast.115) | data formatting | bytes 4194304 | tf_op jit(solution)/shard_map/optimization_barrier | solution.py:104
  44.9 1.6 %fusion.14 = bf16[1024,5,64]{0,1,2:T(8,128)(2,1)} fusion(bf16[8192,2,64]{0,1,2:T(2,128)(2,1)S(1)} %copy.29, s32[]{:T(128)S(6)} %select_n.119, s32[5]{0:T(128)S(1)} %fusion.97), kind=kOutput, calls=%fused_computation.41 | convolution fusion | flops 1638410 | bytes 918020 | tf_op jit(solution)/shard_map/njd,hj->nhd/dot_general | solution.py:44
  46.5 1.5 %fusion.13 = bf16[1024,5,64]{0,1,2:T(8,128)(2,1)} fusion(bf16[8192,2,64]{0,1,2:T(2,128)(2,1)S(1)} %copy.29, s32[]{:T(128)S(6)} %select_n.117, s32[5]{0:T(128)S(1)} %fusion.97), kind=kOutput, calls=%fused_computation.40 | convolution fusion | flops 1638410 | bytes 918020 | tf_op jit(solution)/shard_map/njd,hj->nhd/dot_general | solution.py:44
  48.1 1.5 %fusion.12 = bf16[1024,5,64]{0,1,2:T(8,128)(2,1)} fusion(bf16[8192,2,64]{0,1,2:T(2,128)(2,1)S(1)} %copy.29, s32[]{:T(128)S(6)} %select_n.115, s32[5]{0:T(128)S(1)} %fusion.97), kind=kOutput, calls=%fused_computation.39 | convolution fusion | flops 1638410 | bytes 918020 | tf_op jit(solution)/shard_map/njd,hj->nhd/dot_general | solution.py:44
  50.8 1.6 %fusion.15 = bf16[1024,5,64]{0,1,2:T(8,128)(2,1)S(1)} fusion(bf16[8192,2,64]{0,1,2:T(2,128)(2,1)} %copy-done.5, s32[]{:T(128)S(6)} %select_n.121, s32[5]{0:T(128)S(1)} %fusion.97), kind=kOutput, calls=%fused_computation.42 | convolution fusion | flops 1638410 | bytes 917528 | tf_op jit(solution)/shard_map/njd,hj->nhd/dot_general | solution.py:44
  52.4 2.7 %select_reduce_fusion.1 = (f32[5,256]{1,0:T(8,128)S(1)}, f32[5,1024,256]{2,1,0:T(8,128)S(1)}) fusion(pred[256]{0:T(512)(128)(4,1)S(1)} %get-tuple-element.21, bf16[256,5,64]{0,2,1:T(8,128)(2,1)S(1)} %bitcast.111, bf16[1024,5,64]{0,1,2:T(8,128)(2,1)} %fusion.14), kind=kOutput, calls=%fused_computation.13 | convolution fusion | flops 171703040 | bytes 6067456 | tf_op jit(solution)/shard_map/rhd,phd->hrp/dot_general | solution.py:118
  55.1 1.3 select_reduce_fusion.2
  56.5 1.3 select_reduce_fusion.3
  57.9 1.3 select_reduce_fusion
  59.5 4.4 %bitcast_reduce_fusion.3 = (f32[5,256]{1,0:T(8,128)S(1)}, f32[5,256]{1,0:T(8,128)S(1)}, f32[5,256]{1,0:T(8,128)S(1)}, f32[5,256]{1,0:T(8,128)S(1)}) fusion(f32[5,1024,256]{2,1,0:T(8,128)S(1)} %get-tuple-element.36, f32[5,256]{1,0:T(8,128)S(1)} %maximum_maximum_fusion, pred[256]{0:T(512)(128)(4,1)S(1)} %get-tuple-element.19, ...), kind=kLoop, calls=%fused_computation.6 | loop fusion | flops 20966400 | bytes 20998144 | tf_op jit(solution)/shard_map/reduce_sum | solution.py:149
  64.0 15.0 %all-gather.5.cloned.1.call-done = bf16[8192,2,64]{0,1,2:T(2,128)(2,1)} async-done(((bf16[1024,2,64]{0,1,2:T(2,128)(2,1)}), bf16[8192,2,64]{0,1,2:T(2,128)(2,1)}) %all-gather.5.cloned.1.call-update) | async-done | bytes 2097168 | tf_op jit(solution)/shard_map/all_gather | solution.py:30
  78.9 1.6 %fusion.16 = bf16[1024,5,64]{0,1,2:T(8,128)(2,1)S(1)} fusion(bf16[8192,2,64]{0,1,2:T(2,128)(2,1)} %all-gather.5.cloned.1.call-done, s32[]{:T(128)S(6)} %select_n.115, s32[5]{0:T(128)S(1)} %fusion.97), kind=kOutput, calls=%fused_computation.43 | convolution fusion | flops 1638410 | bytes 917528 | tf_op jit(solution)/shard_map/njd,hj->nhd/dot_general | solution.py:44
  80.6 4.1 %fusion = f32[5,64,256]{2,1,0:T(8,128)S(1)} fusion(f32[5,1024,256]{2,1,0:T(8,128)} %copy-done.4, f32[5,256]{1,0:T(8,128)S(1)} %maximum_maximum_fusion, pred[256]{0:T(512)(128)(4,1)S(1)} %get-tuple-element.19, bf16[1024,5,64]{0,1,2:T(8,128)(2,1)S(1)} %fusion.16), kind=kOutput, calls=%fused_computation.18 | convolution fusion | flops 173015040 | bytes 6231296 | tf_op jit(solution)/shard_map/hrp,phd->rhd/dot_general | solution.py:150
  84.7 1.6 %fusion.17 = bf16[1024,5,64]{0,1,2:T(8,128)(2,1)S(1)} fusion(bf16[8192,2,64]{0,1,2:T(2,128)(2,1)} %all-gather.5.cloned.1.call-done, s32[]{:T(128)S(6)} %select_n.117, s32[5]{0:T(128)S(1)} %fusion.97), kind=kOutput, calls=%fused_computation.44 | convolution fusion | flops 1638410 | bytes 917528 | tf_op jit(solution)/shard_map/njd,hj->nhd/dot_general | solution.py:44
  86.3 1.4 fusion.1
  87.8 1.6 %fusion.18 = bf16[1024,5,64]{0,1,2:T(8,128)(2,1)S(1)} fusion(bf16[8192,2,64]{0,1,2:T(2,128)(2,1)} %all-gather.5.cloned.1.call-done, s32[]{:T(128)S(6)} %select_n.119, s32[5]{0:T(128)S(1)} %fusion.97), kind=kOutput, calls=%fused_computation.45 | convolution fusion | flops 1638410 | bytes 917528 | tf_op jit(solution)/shard_map/njd,hj->nhd/dot_general | solution.py:44
  89.5 1.4 fusion.2
  90.9 1.5 %fusion.19 = bf16[1024,5,64]{0,1,2:T(8,128)(2,1)S(1)} fusion(bf16[8192,2,64]{0,1,2:T(2,128)(2,1)} %all-gather.5.cloned.1.call-done, s32[]{:T(128)S(6)} %select_n.121, s32[5]{0:T(128)S(1)} %fusion.97), kind=kOutput, calls=%fused_computation.46 | convolution fusion | flops 1638410 | bytes 917528 | tf_op jit(solution)/shard_map/njd,hj->nhd/dot_general | solution.py:44
  92.5 1.4 fusion.3
  94.3 1.5 %collective-permute-start = (bf16[256,320]{0,1:T(8,128)(2,1)S(1)}, bf16[256,320]{0,1:T(8,128)(2,1)S(1)}, u32[]{:S(2)}, u32[]{:S(2)}) collective-permute-start(bf16[256,320]{0,1:T(8,128)(2,1)S(1)} %bitcast.118), channel_id=1, source_target_pairs={{0,1},{1,2},{2,3},{3,0},{4,5},{5,6},{6,7},{7,4},{8,9},{9,10},{10,1... | collective-permute-start | bytes 491528 | tf_op jit(solution)/shard_map/ppermute | solution.py:51
  95.8 2.3 %collective-permute-start.4 = (bf16[256,320]{0,1:T(8,128)(2,1)S(1)}, bf16[256,320]{0,1:T(8,128)(2,1)S(1)}, u32[]{:S(2)}, u32[]{:S(2)}) collective-permute-start(bf16[256,320]{0,1:T(8,128)(2,1)S(1)} %bitcast.119), channel_id=1, source_target_pairs={{0,3},{1,0},{2,1},{3,2},{4,7},{5,4},{6,5},{7,6},{8,11},{9,8},{10,9... | collective-permute-start | bytes 491528 | tf_op jit(solution)/shard_map/ppermute | solution.py:51
  100.1 3.1 %collective-permute-done = bf16[256,320]{0,1:T(8,128)(2,1)S(1)} collective-permute-done((bf16[256,320]{0,1:T(8,128)(2,1)S(1)}, bf16[256,320]{0,1:T(8,128)(2,1)S(1)}, u32[]{:S(2)}, u32[]{:S(2)}) %collective-permute-start) | collective-permute-done | bytes 163872 | tf_op jit(solution)/shard_map/ppermute | solution.py:51
  106.7 6.3 %collective-permute-done.2 = bf16[256,320]{0,1:T(8,128)(2,1)S(1)} collective-permute-done((bf16[256,320]{0,1:T(8,128)(2,1)S(1)}, bf16[256,320]{0,1:T(8,128)(2,1)S(1)}, u32[]{:S(2)}, u32[]{:S(2)}) %collective-permute-start.2) | collective-permute-done | bytes 163872 | tf_op jit(solution)/shard_map/ppermute | solution.py:51
  114.1 26.2 %all-gather.7.cloned.1.call-done = bf16[256,2048]{1,0:T(8,128)(2,1)} async-done(((bf16[256,512]{1,0:T(8,128)(2,1)}), bf16[256,2048]{1,0:T(8,128)(2,1)}) %all-gather.7.cloned.1.call-update) | async-done | bytes 1048592 | tf_op jit(solution)/shard_map/all_gather | solution.py:168
  140.4 1.5 fusion.8
  141.9 2.5 %convolution_convert_fusion.10 = bf16[256,320]{0,1:T(8,128)(2,1)} fusion(bf16[2048,320]{0,1:T(8,128)(2,1)S(1)} %copy-done, bf16[256,2048]{1,0:T(8,128)(2,1)} %all-gather.7.cloned.1.call-done, f32[2048]{0:T(1024)S(1)} %convert_element_type.130, f32[256]{0:T(256)S(1)} %add_rsqrt_fusion), kind=kOutput, calls=%fused_computation.65 | convolution fusion | flops 337723392 | bytes 2532352 | tf_op jit(solution)/shard_map/dot_general | solution.py:174
  (75 shorter events, 15.3 us)
Async XLA Ops:
  7.2 134.7 %copy-start = (bf16[2048,320]{0,1:T(8,128)(2,1)S(1)}, bf16[2048,320]{0,1:T(8,128)(2,1)}, u32[]{:S(2)}) copy-start(bf16[2048,320]{0,1:T(8,128)(2,1)} %param.16) | copy-start | bytes 3932164
  7.2 19.3 %copy-start.6 = (bf16[256,320]{0,1:T(8,128)(2,1)S(1)}, bf16[256,320]{0,1:T(8,128)(2,1)}, u32[]{:S(2)}) copy-start(bf16[256,320]{0,1:T(8,128)(2,1)} %param.11) | copy-start | bytes 491524
  7.2 33.9 %all-gather.9.cloned.1.call-start = ((), (), s32[]{:S(2)}) async-start(), calls=%async_computation.2 | async-start | bytes 2359296 | tf_op jit(solution)/shard_map/all_gather | solution.py:30
  9.4 69.6 %all-gather.5.cloned.1.call-start = ((), (), s32[]{:S(2)}) async-start(), calls=%async_computation | async-start | bytes 2359296 | tf_op jit(solution)/shard_map/all_gather | solution.py:30
  11.7 87.8 %collective-permute-start.1 = (bf16[320,512]{1,0:T(8,128)(2,1)}, bf16[320,512]{1,0:T(8,128)(2,1)}, u32[]{:S(2)}, u32[]{:S(2)}) collective-permute-start(bf16[320,512]{1,0:T(8,128)(2,1)} %get-tuple-element.13), channel_id=1, source_target_pairs={{0,1},{1,2},{2,3},{3,0},{4,5},{5,6},{6,7},{7,4},{8,9},{9,10},{10,1... | collective-permute-start | bytes 983048 | tf_op jit(solution)/shard_map/ppermute | solution.py:51
  14.7 89.8 %collective-permute-start.5 = (bf16[320,512]{1,0:T(8,128)(2,1)}, bf16[320,512]{1,0:T(8,128)(2,1)}, u32[]{:S(2)}, u32[]{:S(2)}) collective-permute-start(bf16[320,512]{1,0:T(8,128)(2,1)} %get-tuple-element.14), channel_id=1, source_target_pairs={{0,3},{1,0},{2,1},{3,2},{4,7},{5,4},{6,5},{7,6},{8,11},{9,8},{10,9... | collective-permute-start | bytes 983048 | tf_op jit(solution)/shard_map/ppermute | solution.py:51
  16.7 90.0 %collective-permute-start.3 = (bf16[320,512]{1,0:T(8,128)(2,1)}, bf16[320,512]{1,0:T(8,128)(2,1)S(1)}, u32[]{:S(2)}, u32[]{:S(2)}) collective-permute-start(bf16[320,512]{1,0:T(8,128)(2,1)} %get-tuple-element.12), channel_id=1, source_target_pairs={{0,2},{1,3},{2,0},{3,1},{4,6},{5,7},{6,4},{7,5},{8,10},{9,11},{10,... | collective-permute-start | bytes 983048 | tf_op jit(solution)/shard_map/ppermute | solution.py:51
  44.9 3.2 %copy-start.5 = (bf16[8192,2,64]{0,1,2:T(2,128)(2,1)}, bf16[8192,2,64]{0,1,2:T(2,128)(2,1)S(1)}, u32[]{:S(2)}) copy-start(bf16[8192,2,64]{0,1,2:T(2,128)(2,1)S(1)} %copy.29) | copy-start | bytes 6291460
  50.6 89.8 %all-gather.7.cloned.1.call-start = ((), (), s32[]{:S(2)}) async-start(), calls=%async_computation.1 | async-start | bytes 1310720 | tf_op jit(solution)/shard_map/all_gather | solution.py:168
  50.8 4.3 %copy-start.8 = (bf16[1024,5,64]{0,1,2:T(8,128)(2,1)S(1)}, bf16[1024,5,64]{0,1,2:T(8,128)(2,1)}, u32[]{:S(2)}) copy-start(bf16[1024,5,64]{0,1,2:T(8,128)(2,1)} %fusion.13) | copy-start | bytes 1966084
  52.4 4.1 %copy-start.7 = (bf16[1024,5,64]{0,1,2:T(8,128)(2,1)S(1)}, bf16[1024,5,64]{0,1,2:T(8,128)(2,1)}, u32[]{:S(2)}) copy-start(bf16[1024,5,64]{0,1,2:T(8,128)(2,1)} %fusion.12) | copy-start | bytes 1966084
  55.1 4.4 %copy-start.1 = (f32[5,1024,256]{2,1,0:T(8,128)}, f32[5,1024,256]{2,1,0:T(8,128)S(1)}, u32[]{:S(2)}) copy-start(f32[5,1024,256]{2,1,0:T(8,128)S(1)} %get-tuple-element.30) | copy-start | bytes 15728644
  56.5 3.0 %copy-start.3 = (f32[5,1024,256]{2,1,0:T(8,128)}, f32[5,1024,256]{2,1,0:T(8,128)S(1)}, u32[]{:S(2)}) copy-start(f32[5,1024,256]{2,1,0:T(8,128)S(1)} %get-tuple-element.32) | copy-start | bytes 15728644
  57.9 6.1 %copy-start.4 = (f32[5,1024,256]{2,1,0:T(8,128)}, f32[5,1024,256]{2,1,0:T(8,128)S(1)}, u32[]{:S(2)}) copy-start(f32[5,1024,256]{2,1,0:T(8,128)S(1)} %get-tuple-element.36) | copy-start | bytes 15728644
  59.2 4.7 %copy-start.2 = (f32[5,1024,256]{2,1,0:T(8,128)}, f32[5,1024,256]{2,1,0:T(8,128)S(1)}, u32[]{:S(2)}) copy-start(f32[5,1024,256]{2,1,0:T(8,128)S(1)} %get-tuple-element.28) | copy-start | bytes 15728644
  78.9 7.4 %slice-start.4 = ((s8[5242880]{0:T(1024)(128)(4,1)}), s8[4194304]{0:T(1024)(128)(4,1)S(1)}, s32[]{:S(2)}) async-start(s8[5242880]{0:T(1024)(128)(4,1)} %bitcast.108), calls=%async_computation.7 | async-start | bytes 8388608
  80.6 5.7 %slice-start.5 = ((s8[5242880]{0:T(1024)(128)(4,1)}), s8[1048576]{0:T(1024)(128)(4,1)S(1)}, s32[]{:S(2)}) async-start(s8[5242880]{0:T(1024)(128)(4,1)} %bitcast.108), calls=%async_computation.8 | async-start | bytes 2097152
  84.7 4.8 %slice-start = ((s8[5242880]{0:T(1024)(128)(4,1)}), s8[4194304]{0:T(1024)(128)(4,1)S(1)}, s32[]{:S(2)}) async-start(s8[5242880]{0:T(1024)(128)(4,1)} %bitcast.104), calls=%async_computation.3 | async-start | bytes 8388608
  86.3 3.1 %slice-start.1 = ((s8[5242880]{0:T(1024)(128)(4,1)}), s8[1048576]{0:T(1024)(128)(4,1)S(1)}, s32[]{:S(2)}) async-start(s8[5242880]{0:T(1024)(128)(4,1)} %bitcast.104), calls=%async_computation.4 | async-start | bytes 2097152
  87.8 4.6 %slice-start.2 = ((s8[5242880]{0:T(1024)(128)(4,1)}), s8[4194304]{0:T(1024)(128)(4,1)S(1)}, s32[]{:S(2)}) async-start(s8[5242880]{0:T(1024)(128)(4,1)} %bitcast.106), calls=%async_computation.5 | async-start | bytes 8388608
  89.4 3.0 %slice-start.3 = ((s8[5242880]{0:T(1024)(128)(4,1)}), s8[1048576]{0:T(1024)(128)(4,1)S(1)}, s32[]{:S(2)}) async-start(s8[5242880]{0:T(1024)(128)(4,1)} %bitcast.106), calls=%async_computation.6 | async-start | bytes 2097152
  90.9 3.0 %copy-start.9 = (bf16[256,5,64]{0,1,2:T(8,128)(2,1)S(1)}, bf16[256,5,64]{0,1,2:T(8,128)(2,1)}, u32[]{:S(2)}) copy-start(bf16[256,5,64]{0,1,2:T(8,128)(2,1)} %fusion.28) | copy-start | bytes 491524
  93.9 19.1 %copy-start.10 = (bf16[256,512]{1,0:T(8,128)(2,1)S(1)}, bf16[256,512]{1,0:T(8,128)(2,1)}, u32[]{:S(2)}) copy-start(bf16[256,512]{1,0:T(8,128)(2,1)} %param.10) | copy-start | bytes 786436
  93.9 20.2 %copy-start.11 = (bf16[2048]{0:T(1024)(128)(2,1)S(1)}, bf16[2048]{0:T(1024)(128)(2,1)}, u32[]{:S(2)}) copy-start(bf16[2048]{0:T(1024)(128)(2,1)} %param.15) | copy-start | bytes 12292
  94.3 8.9 %collective-permute-start = (bf16[256,320]{0,1:T(8,128)(2,1)S(1)}, bf16[256,320]{0,1:T(8,128)(2,1)S(1)}, u32[]{:S(2)}, u32[]{:S(2)}) collective-permute-start(bf16[256,320]{0,1:T(8,128)(2,1)S(1)} %bitcast.118), channel_id=1, source_target_pairs={{0,1},{1,2},{2,3},{3,0},{4,5},{5,6},{6,7},{7,4},{8,9},{9,10},{10,1... | collective-permute-start | bytes 491528 | tf_op jit(solution)/shard_map/ppermute | solution.py:51
  95.8 9.6 %collective-permute-start.4 = (bf16[256,320]{0,1:T(8,128)(2,1)S(1)}, bf16[256,320]{0,1:T(8,128)(2,1)S(1)}, u32[]{:S(2)}, u32[]{:S(2)}) collective-permute-start(bf16[256,320]{0,1:T(8,128)(2,1)S(1)} %bitcast.119), channel_id=1, source_target_pairs={{0,3},{1,0},{2,1},{3,2},{4,7},{5,4},{6,5},{7,6},{8,11},{9,8},{10,9... | collective-permute-start | bytes 491528 | tf_op jit(solution)/shard_map/ppermute | solution.py:51
  99.5 13.6 %collective-permute-start.2 = (bf16[256,320]{0,1:T(8,128)(2,1)S(1)}, bf16[256,320]{0,1:T(8,128)(2,1)S(1)}, u32[]{:S(2)}, u32[]{:S(2)}) collective-permute-start(bf16[256,320]{0,1:T(8,128)(2,1)S(1)} %bitcast.121), channel_id=1, source_target_pairs={{0,2},{1,3},{2,0},{3,1},{4,6},{5,7},{6,4},{7,5},{8,10},{9,11},{10,... | collective-permute-start | bytes 491528 | tf_op jit(solution)/shard_map/ppermute | solution.py:51
Sparse Core Ops, SparseCore 0:
  10.5 30.5 all-gather.8
  50.7 28.1 all-gather.4
  114.2 26.1 all-gather.6
where the time goes:
time: 151 us
  waiting for transfers between devices  65.7 us (44%)
  matrix products  37.2 us (25%)
  between operations  16.9 us (11%)
  local copies, waits for them, and re-layouts  11.6 us (8%)
  starting transfers between devices  10.9 us (7%)
  other arithmetic  8.57 us (6%)
    all_gather x2, waiting for transfers between devices, every_slot_of(): return lax.all_gather(part, 'req', axis=0, tiled=True)  29.2 us
    all_gather x1, waiting for transfers between devices, local(): full_new = lax.all_gather(new_residual, 'tp', axis=1, tiled=True)  26.2 us
    dot_general x8, matrix products, pick_part(): jnp.einsum('njd,hj->nhd', part_rows, select, preferred_element_type=jnp.f...  12.6 us
    ppermute x6, starting transfers between devices, shifted(): return lax.ppermute(block, 'tp', pairs)  10.6 us
    ppermute x6, waiting for transfers between devices, shifted(): return lax.ppermute(block, 'tp', pairs)  10.3 us
    dot_general x4, matrix products, local(): jnp.einsum('hrp,phd->rhd', prefix_weights.astype(jnp.bfloat16), picked[te...  8.43 us
    dot_general x4, matrix products, local(): jnp.einsum('rhd,phd->hrp', query_heads, picked[tenant_id][0], preferred_e...  6.74 us
    optimization_barrier x2, local copies, waits for them, and re-layouts, local(): own_values, every_key = lax.optimization_barrier((own_values, every_key))  4.73 us
  transfers between devices with their start and end apart: 9, of which 6 were waited for; matrix products, arithmetic and copies ran while one was open for 33% of the time, Pallas kernels for 0%

commit v1 on v0

--- a/solution.py
+++ b/solution.py
@@ -8,6 +8,18 @@
 HD = 64
 TENANTS = 4
 GATHER_SLOTS_MAX = 16
+
+
+def collect(x, axis, dim):
+    ways, here, hop = (lax.axis_size(axis), lax.axis_index(axis), x.shape[dim])
+    line, have = (x, 1)
+    while have < ways:
+        line = jnp.concatenate(
+            [line, lax.ppermute(line, axis, [(d, (d - have) % ways) for d in range(ways)])],
+            axis=dim,
+        )
+        have = 2 * have
+    return jnp.roll(line, here * hop, axis=dim)
 
 
 def from_root(block, axis, source):
@@ -27,7 +39,7 @@
 
 
 def every_slot_of(part, n_req):
-    return lax.all_gather(part, "req", axis=0, tiled=True)
+    return collect(part, "req", 0)
 
 
 def slots_of_tenants(part, every_slot, owners, n_req):

time: 151 us -> 209 us (1.38)
  waiting for transfers between devices: 65.7 us -> 101 us
  other arithmetic: 8.57 us -> 41.6 us
  matrix products: 37.2 us -> 24.1 us
  starting transfers between devices: 10.9 us -> 20 us
  local copies, waits for them, and re-layouts: 11.6 us -> 4.8 us
    ppermute x0 -> x6, waiting for transfers between devices: none -> 62.4 us  [collect(): lax.ppermute(line, axis, [(d, (d - have) % ways) for d in range(ways)])]
    concatenate x0 -> x6, other arithmetic: none -> 35.2 us  [the longest x2 31.8 us: collect(): return jnp.roll(line, here * hop, axis=dim)]
    all_gather x2 -> x0, waiting for transfers between devices: 29.2 us -> none  [every_slot_of(): return lax.all_gather(part, 'req', axis=0, tiled=True)]
    ppermute x0 -> x6, starting transfers between devices: none -> 10.3 us  [collect(): lax.ppermute(line, axis, [(d, (d - have) % ways) for d in range(ways)])]
    dot_general x8, matrix products: 12.6 us -> 5.14 us  [pick_part(): jnp.einsum('njd,hj->nhd', part_rows, select, preferred_element_type=jnp.f...]
    optimization_barrier x2 -> x1, local copies, waits for them, and re-layouts: 4.73 us -> 0.27 us  [local(): own_values, every_key = lax.optimization_barrier((own_values, every_key))]
    dot_general x4, matrix products: 8.43 us -> 5.75 us  [local(): jnp.einsum('hrp,phd->rhd', prefix_weights.astype(jnp.bfloat16), picked[te...]
  transfers between devices with their start and end apart: 9 -> 13, of which waited for: 6 -> 7; matrix products, arithmetic and copies ran while one was open for 33% -> 30% of each run, Pallas kernels for 0% -> 0%
where the time goes in v1:
time: 209 us
  waiting for transfers between devices  101 us (48%)
  other arithmetic  41.6 us (20%)
  matrix products  24.1 us (12%)
  starting transfers between devices  20 us (10%)
  between operations  17.1 us (8%)
  local copies, waits for them, and re-layouts  4.8 us (2%)
    ppermute x6, waiting for transfers between devices, collect(): lax.ppermute(line, axis, [(d, (d - have) % ways) for d in range(ways)])  62.4 us
    concatenate x2, other arithmetic, collect(): return jnp.roll(line, here * hop, axis=dim)  31.8 us
    all_gather x1, waiting for transfers between devices, local(): full_new = lax.all_gather(new_residual, 'tp', axis=1, tiled=True)  28.1 us
    ppermute x6, waiting for transfers between devices, shifted(): return lax.ppermute(block, 'tp', pairs)  10.8 us
    ppermute x6, starting transfers between devices, collect(): lax.ppermute(line, axis, [(d, (d - have) % ways) for d in range(ways)])  10.3 us
    ppermute x6, starting transfers between devices, shifted(): return lax.ppermute(block, 'tp', pairs)  9.68 us
    dot_general x4, matrix products, local(): jnp.einsum('hrp,phd->rhd', prefix_weights.astype(jnp.bfloat16), picked[te...  5.75 us
    dot_general x4, matrix products, local(): jnp.einsum('rhd,phd->hrp', query_heads, picked[tenant_id][0], preferred_e...  5.44 us
  transfers between devices with their start and end apart: 13, of which 7 were waited for; matrix products, arithmetic and copies ran while one was open for 30% of the time, Pallas kernels for 0%

profile of v1, /device:TPU:0, one launch (start us, length us, event | category | flops | bytes accessed | tf_op | source)
XLA Modules:
  0.0 208.9 jit_solution(6750652401001016375)
XLA Ops:
  7.3 1.3 copy.28
  8.9 3.4 %collective-permute-start = (bf16[1024,2,64]{0,1,2:T(2,128)(2,1)S(1)}, bf16[1024,2,64]{0,1,2:T(2,128)(2,1)S(1)}, u32[]{:S(2)}, u32[]{:S(2)}) collective-permute-start(bf16[1024,2,64]{0,1,2:T(2,128)(2,1)S(1)} %copy.32), channel_id=1, source_target_pairs={{0,28},{4,0},{8,4},{12,8},{16,12},{20,16},{24,20},{28,24},{1,29},{... | collective-permute-start | bytes 786440 | tf_op jit(solution)/shard_map/ppermute | solution.py:18
  12.3 2.1 constant_dynamic-slice_fusion.1
  14.4 3.6 %collective-permute-start.11 = (bf16[320,512]{1,0:T(8,128)(2,1)}, bf16[320,512]{1,0:T(8,128)(2,1)S(1)}, u32[]{:S(2)}, u32[]{:S(2)}) collective-permute-start(bf16[320,512]{1,0:T(8,128)(2,1)} %get-tuple-element.15), channel_id=1, source_target_pairs={{0,3},{1,0},{2,1},{3,2},{4,7},{5,4},{6,5},{7,6},{8,11},{9,8},{10,9... | collective-permute-start | bytes 983048 | tf_op jit(solution)/shard_map/ppermute | solution.py:63
  24.0 10.8 %collective-permute-done.1 = bf16[2048,2,64]{0,1,2:T(2,128)(2,1)S(1)} collective-permute-done((bf16[2048,2,64]{0,1,2:T(2,128)(2,1)S(1)}, bf16[2048,2,64]{0,1,2:T(2,128)(2,1)S(1)}, u32[]{:S(2)}, u32[]{:S(2)}) %collective-permute-start.1) | collective-permute-done | bytes 524320 | tf_op jit(solution)/shard_map/ppermute | solution.py:18
  34.8 1.3 pad_maximum_fusion
  36.1 1.6 collective-permute-start.2
  38.7 21.2 %collective-permute-done.2 = bf16[4096,2,64]{0,1,2:T(2,128)(2,1)S(1)} collective-permute-done((bf16[4096,2,64]{0,1,2:T(2,128)(2,1)S(1)}, bf16[4096,2,64]{0,1,2:T(2,128)(2,1)S(1)}, u32[]{:S(2)}, u32[]{:S(2)}) %collective-permute-start.2) | collective-permute-done | bytes 1048608 | tf_op jit(solution)/shard_map/ppermute | solution.py:18
  59.9 13.7 %fusion.17 = bf16[8192,2,64]{0,1,2:T(2,128)(2,1)S(1)} fusion(s32[]{:T(128)S(6)} %select_n.152, bf16[4096,2,64]{0,1,2:T(2,128)(2,1)S(1)} %collective-permute-done.2, bf16[2048,2,64]{0,1,2:T(2,128)(2,1)S(1)} %collective-permute-done.1, bf16[1024,2,64]{0,1,2:T(2,128)(2,1)S(1)} %collective-permute-done, bf16[1024,2,64]{0,1,2:T(2,128)(2,1)S(1)} %copy.32), kind=kLoop, calls=%fused_computation.44 | loop fusion | flops 16777216 | bytes 4194308 | tf_op jit(solution)/shard_map/jit(_roll_dynamic)/concatenate | solution.py:22
  76.5 1.3 select_reduce_fusion
  77.8 1.3 select_reduce_fusion.1
  79.2 1.4 select_reduce_fusion.2
  81.6 2.7 %collective-permute-start.4 = (bf16[2048,2,64]{0,1,2:T(2,128)(2,1)S(1)}, bf16[2048,2,64]{0,1,2:T(2,128)(2,1)S(1)}, u32[]{:S(2)}, u32[]{:S(2)}) collective-permute-start(bf16[2048,2,64]{0,1,2:T(2,128)(2,1)S(1)} %pad_maximum_fusion.3), channel_id=1, source_target_pairs={{0,24},{4,28},{8,0},{12,4},{16,8},{20,12},{24,16},{28,20},{1,25},{... | collective-permute-start | bytes 1572872 | tf_op jit(solution)/shard_map/ppermute | solution.py:18
  84.3 1.4 select_reduce_fusion.3
  85.9 10.3 %collective-permute-done.4 = bf16[2048,2,64]{0,1,2:T(2,128)(2,1)S(1)} collective-permute-done((bf16[2048,2,64]{0,1,2:T(2,128)(2,1)S(1)}, bf16[2048,2,64]{0,1,2:T(2,128)(2,1)S(1)}, u32[]{:S(2)}, u32[]{:S(2)}) %collective-permute-start.4) | collective-permute-done | bytes 524320 | tf_op jit(solution)/shard_map/ppermute | solution.py:18
  96.2 1.2 pad_maximum_fusion.1
  98.4 4.1 %bitcast_reduce_fusion.3 = (f32[5,256]{1,0:T(8,128)S(1)}, f32[5,256]{1,0:T(8,128)S(1)}, f32[5,256]{1,0:T(8,128)S(1)}, f32[5,256]{1,0:T(8,128)S(1)}) fusion(f32[5,1024,256]{2,1,0:T(8,128)S(1)} %get-tuple-element.37, f32[5,256]{1,0:T(8,128)S(1)} %maximum_maximum_fusion.1, pred[256]{0:T(512)(128)(4,1)S(1)} %get-tuple-element.20, ...), kind=kLoop, calls=%fused_computation.6 | loop fusion | flops 20966400 | bytes 20998144 | tf_op jit(solution)/shard_map/reduce_sum | solution.py:161
  102.5 20.1 %collective-permute-done.5 = bf16[4096,2,64]{0,1,2:T(2,128)(2,1)S(1)} collective-permute-done((bf16[4096,2,64]{0,1,2:T(2,128)(2,1)S(1)}, bf16[4096,2,64]{0,1,2:T(2,128)(2,1)S(1)}, u32[]{:S(2)}, u32[]{:S(2)}) %collective-permute-start.5) | collective-permute-done | bytes 1048608 | tf_op jit(solution)/shard_map/ppermute | solution.py:18
  122.7 18.1 %maximum_maximum_fusion = bf16[16384,2,64]{0,1,2:T(2,128)(2,1)S(1)} fusion(bf16[4096,2,64]{0,1,2:T(2,128)(2,1)S(1)} %collective-permute-done.5, bf16[2048,2,64]{0,1,2:T(2,128)(2,1)S(1)} %collective-permute-done.4, bf16[1024,2,64]{0,1,2:T(2,128)(2,1)S(1)} %collective-permute-done.3, bf16[1024,2,64]{0,1,2:T(2,128)(2,1)S(1)} %copy.42), kind=kLoop, calls=%fused_computation.24 | loop fusion | flops 33554432 | bytes 6291456 | tf_op jit(solution)/shard_map/jit(_roll_dynamic)/concatenate | solution.py:22
  141.5 1.4 fusion.3
  143.8 1.4 fusion.2
  146.0 1.4 fusion.1
  148.2 1.4 fusion
  150.0 3.9 %collective-permute-start.10 = (bf16[256,320]{0,1:T(8,128)(2,1)S(1)}, bf16[256,320]{0,1:T(8,128)(2,1)S(1)}, u32[]{:S(2)}, u32[]{:S(2)}) collective-permute-start(bf16[256,320]{0,1:T(8,128)(2,1)S(1)} %bitcast.112), channel_id=1, source_target_pairs={{0,3},{1,0},{2,1},{3,2},{4,7},{5,4},{6,5},{7,6},{8,11},{9,8},{10,9... | collective-permute-start | bytes 491528 | tf_op jit(solution)/shard_map/ppermute | solution.py:63
  153.8 1.3 fusion.59
  155.1 1.2 collective-permute-start.8
  156.3 6.5 %collective-permute-done.6 = bf16[256,320]{0,1:T(8,128)(2,1)S(1)} collective-permute-done((bf16[256,320]{0,1:T(8,128)(2,1)S(1)}, bf16[256,320]{0,1:T(8,128)(2,1)S(1)}, u32[]{:S(2)}, u32[]{:S(2)}) %collective-permute-start.6) | collective-permute-done | bytes 163872 | tf_op jit(solution)/shard_map/ppermute | solution.py:63
  162.9 1.3 convolution_add_fusion.1
  164.5 4.2 %collective-permute-done.8 = bf16[256,320]{0,1:T(8,128)(2,1)S(1)} collective-permute-done((bf16[256,320]{0,1:T(8,128)(2,1)S(1)}, bf16[256,320]{0,1:T(8,128)(2,1)S(1)}, u32[]{:S(2)}, u32[]{:S(2)}) %collective-permute-start.8) | collective-permute-done | bytes 163872 | tf_op jit(solution)/shard_map/ppermute | solution.py:63
  169.9 28.1 %all-gather.2.cloned.1.call-done = bf16[256,2048]{1,0:T(8,128)(2,1)} async-done(((bf16[256,512]{1,0:T(8,128)(2,1)}), bf16[256,2048]{1,0:T(8,128)(2,1)}) %all-gather.2.cloned.1.call-update) | async-done | bytes 1048592 | tf_op jit(solution)/shard_map/all_gather | solution.py:180
  198.0 1.5 fusion.14
  199.5 2.5 %convolution_convert_fusion.10 = bf16[256,320]{0,1:T(8,128)(2,1)} fusion(bf16[2048,320]{0,1:T(8,128)(2,1)S(1)} %copy-done, bf16[256,2048]{1,0:T(8,128)(2,1)} %all-gather.2.cloned.1.call-done, f32[2048]{0:T(1024)S(1)} %convert_element_type.130, f32[256]{0:T(256)S(1)} %add_rsqrt_fusion), kind=kOutput, calls=%fused_computation.81 | convolution fusion | flops 337723392 | bytes 2532352 | tf_op jit(solution)/shard_map/dot_general | solution.py:186
  (64 shorter events, 14.5 us)
Async XLA Ops:
  7.2 192.3 %copy-start = (bf16[2048,320]{0,1:T(8,128)(2,1)S(1)}, bf16[2048,320]{0,1:T(8,128)(2,1)}, u32[]{:S(2)}) copy-start(bf16[2048,320]{0,1:T(8,128)(2,1)} %param.18) | copy-start | bytes 3932164
  7.2 11.8 %copy-start.7 = (s32[1,4]{1,0:T(1,128)S(1)}, s32[1,4]{1,0:T(1,128)}, u32[]{:S(2)}) copy-start(s32[1,4]{1,0:T(1,128)} %param.19) | copy-start | bytes 52
  7.2 12.1 %copy-start.4 = (s32[4]{0:T(128)S(1)}, s32[4]{0:T(128)}, u32[]{:S(2)}) copy-start(s32[4]{0:T(128)} %param.21) | copy-start | bytes 52
  7.2 15.3 %copy-start.3 = (bf16[256,1,256]{2,0,1:T(8,128)(2,1)S(1)}, bf16[256,1,256]{2,0,1:T(8,128)(2,1)}, u32[]{:S(2)}) copy-start(bf16[256,1,256]{2,0,1:T(8,128)(2,1)} %param.14) | copy-start | bytes 393220
  7.2 16.6 %copy-start.6 = (s32[1,4]{1,0:T(1,128)S(1)}, s32[1,4]{1,0:T(1,128)}, u32[]{:S(2)}) copy-start(s32[1,4]{1,0:T(1,128)} %param.20) | copy-start | bytes 52
  7.2 190.8 %all-gather.2.cloned.1.call-start = ((), (), s32[]{:S(2)}) async-start(), calls=%async_computation | async-start | bytes 1310720 | tf_op jit(solution)/shard_map/all_gather | solution.py:180
  8.6 29.7 %copy-start.1 = (bf16[256,320]{0,1:T(8,128)(2,1)S(1)}, bf16[256,320]{0,1:T(8,128)(2,1)}, u32[]{:S(2)}) copy-start(bf16[256,320]{0,1:T(8,128)(2,1)} %param.13) | copy-start | bytes 491524
  8.9 13.7 %collective-permute-start = (bf16[1024,2,64]{0,1,2:T(2,128)(2,1)S(1)}, bf16[1024,2,64]{0,1,2:T(2,128)(2,1)S(1)}, u32[]{:S(2)}, u32[]{:S(2)}) collective-permute-start(bf16[1024,2,64]{0,1,2:T(2,128)(2,1)S(1)} %copy.32), channel_id=1, source_target_pairs={{0,28},{4,0},{8,4},{12,8},{16,12},{20,16},{24,20},{28,24},{1,29},{... | collective-permute-start | bytes 786440 | tf_op jit(solution)/shard_map/ppermute | solution.py:18
  14.4 149.8 %collective-permute-start.11 = (bf16[320,512]{1,0:T(8,128)(2,1)}, bf16[320,512]{1,0:T(8,128)(2,1)S(1)}, u32[]{:S(2)}, u32[]{:S(2)}) collective-permute-start(bf16[320,512]{1,0:T(8,128)(2,1)} %get-tuple-element.15), channel_id=1, source_target_pairs={{0,3},{1,0},{2,1},{3,2},{4,7},{5,4},{6,5},{7,6},{8,11},{9,8},{10,9... | collective-permute-start | bytes 983048 | tf_op jit(solution)/shard_map/ppermute | solution.py:63
  18.0 137.1 %collective-permute-start.7 = (bf16[320,512]{1,0:T(8,128)(2,1)}, bf16[320,512]{1,0:T(8,128)(2,1)}, u32[]{:S(2)}, u32[]{:S(2)}) collective-permute-start(bf16[320,512]{1,0:T(8,128)(2,1)} %get-tuple-element.14), channel_id=1, source_target_pairs={{0,1},{1,2},{2,3},{3,0},{4,5},{5,6},{6,7},{7,4},{8,9},{9,10},{10,1... | collective-permute-start | bytes 983048 | tf_op jit(solution)/shard_map/ppermute | solution.py:63
  18.0 146.5 %collective-permute-start.9 = (bf16[320,512]{1,0:T(8,128)(2,1)S(1)}, bf16[320,512]{1,0:T(8,128)(2,1)S(1)}, u32[]{:S(2)}, u32[]{:S(2)}) collective-permute-start(bf16[320,512]{1,0:T(8,128)(2,1)S(1)} %get-tuple-element.13), channel_id=1, source_target_pairs={{0,2},{1,3},{2,0},{3,1},{4,6},{5,7},{6,4},{7,5},{8,10},{9,11},{10,... | collective-permute-start | bytes 983048 | tf_op jit(solution)/shard_map/ppermute | solution.py:63
  23.2 11.7 %collective-permute-start.1 = (bf16[2048,2,64]{0,1,2:T(2,128)(2,1)S(1)}, bf16[2048,2,64]{0,1,2:T(2,128)(2,1)S(1)}, u32[]{:S(2)}, u32[]{:S(2)}) collective-permute-start(bf16[2048,2,64]{0,1,2:T(2,128)(2,1)S(1)} %pad_maximum_fusion.2), channel_id=1, source_target_pairs={{0,24},{4,28},{8,0},{12,4},{16,8},{20,12},{24,16},{28,20},{1,25},{... | collective-permute-start | bytes 1572872 | tf_op jit(solution)/shard_map/ppermute | solution.py:18
  36.1 23.8 %collective-permute-start.2 = (bf16[4096,2,64]{0,1,2:T(2,128)(2,1)S(1)}, bf16[4096,2,64]{0,1,2:T(2,128)(2,1)S(1)}, u32[]{:S(2)}, u32[]{:S(2)}) collective-permute-start(bf16[4096,2,64]{0,1,2:T(2,128)(2,1)S(1)} %pad_maximum_fusion), channel_id=1, source_target_pairs={{0,16},{4,20},{8,24},{12,28},{16,0},{20,4},{24,8},{28,12},{1,17},{... | collective-permute-start | bytes 3145736 | tf_op jit(solution)/shard_map/ppermute | solution.py:18
  75.5 5.6 %collective-permute-start.3 = (bf16[1024,2,64]{0,1,2:T(2,128)(2,1)S(1)}, bf16[1024,2,64]{0,1,2:T(2,128)(2,1)S(1)}, u32[]{:S(2)}, u32[]{:S(2)}) collective-permute-start(bf16[1024,2,64]{0,1,2:T(2,128)(2,1)S(1)} %copy.42), channel_id=1, source_target_pairs={{0,28},{4,0},{8,4},{12,8},{16,12},{20,16},{24,20},{28,24},{1,29},{... | collective-permute-start | bytes 786440 | tf_op jit(solution)/shard_map/ppermute | solution.py:18
  81.6 14.6 %collective-permute-start.4 = (bf16[2048,2,64]{0,1,2:T(2,128)(2,1)S(1)}, bf16[2048,2,64]{0,1,2:T(2,128)(2,1)S(1)}, u32[]{:S(2)}, u32[]{:S(2)}) collective-permute-start(bf16[2048,2,64]{0,1,2:T(2,128)(2,1)S(1)} %pad_maximum_fusion.3), channel_id=1, source_target_pairs={{0,24},{4,28},{8,0},{12,4},{16,8},{20,12},{24,16},{28,20},{1,25},{... | collective-permute-start | bytes 1572872 | tf_op jit(solution)/shard_map/ppermute | solution.py:18
  97.4 25.2 %collective-permute-start.5 = (bf16[4096,2,64]{0,1,2:T(2,128)(2,1)S(1)}, bf16[4096,2,64]{0,1,2:T(2,128)(2,1)S(1)}, u32[]{:S(2)}, u32[]{:S(2)}) collective-permute-start(bf16[4096,2,64]{0,1,2:T(2,128)(2,1)S(1)} %pad_maximum_fusion.1), channel_id=1, source_target_pairs={{0,16},{4,20},{8,24},{12,28},{16,0},{20,4},{24,8},{28,12},{1,17},{... | collective-permute-start | bytes 3145736 | tf_op jit(solution)/shard_map/ppermute | solution.py:18
  149.6 19.2 %copy-start.2 = (bf16[256,512]{1,0:T(8,128)(2,1)S(1)}, bf16[256,512]{1,0:T(8,128)(2,1)}, u32[]{:S(2)}) copy-start(bf16[256,512]{1,0:T(8,128)(2,1)} %param.12) | copy-start | bytes 786436
  149.6 20.2 %copy-start.5 = (bf16[2048]{0:T(1024)(128)(2,1)S(1)}, bf16[2048]{0:T(1024)(128)(2,1)}, u32[]{:S(2)}) copy-start(bf16[2048]{0:T(1024)(128)(2,1)} %param.17) | copy-start | bytes 12292
  150.0 14.2 %collective-permute-start.10 = (bf16[256,320]{0,1:T(8,128)(2,1)S(1)}, bf16[256,320]{0,1:T(8,128)(2,1)S(1)}, u32[]{:S(2)}, u32[]{:S(2)}) collective-permute-start(bf16[256,320]{0,1:T(8,128)(2,1)S(1)} %bitcast.112), channel_id=1, source_target_pairs={{0,3},{1,0},{2,1},{3,2},{4,7},{5,4},{6,5},{7,6},{8,11},{9,8},{10,9... | collective-permute-start | bytes 491528 | tf_op jit(solution)/shard_map/ppermute | solution.py:63
  153.8 9.0 %collective-permute-start.6 = (bf16[256,320]{0,1:T(8,128)(2,1)S(1)}, bf16[256,320]{0,1:T(8,128)(2,1)S(1)}, u32[]{:S(2)}, u32[]{:S(2)}) collective-permute-start(bf16[256,320]{0,1:T(8,128)(2,1)S(1)} %bitcast.113), channel_id=1, source_target_pairs={{0,1},{1,2},{2,3},{3,0},{4,5},{5,6},{6,7},{7,4},{8,9},{9,10},{10,1... | collective-permute-start | bytes 491528 | tf_op jit(solution)/shard_map/ppermute | solution.py:63
  155.1 13.6 %collective-permute-start.8 = (bf16[256,320]{0,1:T(8,128)(2,1)S(1)}, bf16[256,320]{0,1:T(8,128)(2,1)S(1)}, u32[]{:S(2)}, u32[]{:S(2)}) collective-permute-start(bf16[256,320]{0,1:T(8,128)(2,1)S(1)} %bitcast.115), channel_id=1, source_target_pairs={{0,2},{1,3},{2,0},{3,1},{4,6},{5,7},{6,4},{7,5},{8,10},{9,11},{10,... | collective-permute-start | bytes 491528 | tf_op jit(solution)/shard_map/ppermute | solution.py:63
Sparse Core Ops, SparseCore 0:
  170.0 27.9 all-gather.1
